TPU v7x, 256 devices: a whole 4x4x8 slice. The times are simulated.
256 devices in a mesh: member: 8 (over x, y_hi), space: 32 (over y_lo, z, core).
Axes of the slice: x: 4, y: 4 (y_hi: 2, y_lo: 2; y = y_hi * 2 + y_lo), z: 8, core: 2. Of those that a mesh axis runs over, the one named last changes fastest.
Arguments:
- ensemble: bfloat16 [256, 48, 16384], P('member', None, 'space')
- inflation: float32 [256, 128], P('member'), may hold values from 0.5 to 2
- weights: bfloat16 [128, 256, 256], P('space')
- region_ids: int32 [16384], P('space'), may hold values from 0 to 127, as said below
- extinction: float32 [48], replicated, may hold values from 0.1 to 2
- obs_cols: int32 [4096], P('space'), may hold values from 0 to 16383, as said below
Outputs:
- analysis: bfloat16 [256, 48, 16384], P('member', None, 'space')
- obs_analysis: float32 [256, 4096], P('member', 'space')
Inputs may be any that keep to these rules, and one draw needn't show every extreme that they name: `region_ids`: region r belongs to index r // 4 of space. Each block of 512 columns held by one index of space holds exactly 16 columns of the regions of every index of space. `obs_cols`: each observation's column lies in the block of 512 columns held by the same index of space as the observation.
All inputs are finite; a program needn't handle non-finite values.
Results may differ from a plain program's by a relative error of at most 0.0047.
Values may be sent and summed in bfloat16 or wider, within the bound.
No kernel may reach another device: no remote copies, remote signals or barrier semaphores. Data moves between devices by JAX's collectives and lax.ppermute only.
A program may use at most 64 MiB of HBM per device.

v0:
```python
import jax
import jax.numpy as jnp
from jax import lax
from jax.sharding import PartitionSpec as P


def _split3(x):
    hi = lax.reduce_precision(x, exponent_bits=8, mantissa_bits=7)
    r1 = x - hi
    mid = lax.reduce_precision(r1, exponent_bits=8, mantissa_bits=7)
    lo = r1 - mid
    return (hi.astype(jnp.bfloat16), mid.astype(jnp.bfloat16), lo.astype(jnp.bfloat16))


def local(ensemble, inflation, weights, region_ids, extinction, obs_cols):
    n_space = lax.axis_size("space")
    n_member = lax.axis_size("member")
    local_members = ensemble.shape[0]
    tracers = ensemble.shape[1]
    columns = ensemble.shape[2]
    members = local_members * n_member
    reg_count = weights.shape[0]
    all_regions = inflation.shape[1]
    send_cols = columns // n_space
    slot_cols = send_cols // n_member
    own_cols = n_space * slot_cols
    row_len = local_members * tracers
    extra_len = 128
    owner = region_ids // reg_count
    owner_hot = (owner[:, None] == jnp.arange(n_space, dtype=jnp.int32)[None, :]).astype(jnp.int32)
    before = jnp.cumsum(owner_hot, axis=0) - owner_hot
    rank_in = jnp.sum(before * owner_hot, axis=1)
    position = owner * send_cols + rank_in
    ordering = (
        jnp.zeros((columns,), jnp.int32).at[position].set(jnp.arange(columns, dtype=jnp.int32))
    )
    region_hot = (jnp.arange(all_regions, dtype=jnp.int32)[:, None] == region_ids[None, :]).astype(
        jnp.float32
    )
    factor = jnp.dot(inflation, region_hot, precision=lax.Precision.HIGHEST)
    f_hi, f_mid, f_lo = _split3(factor.T)
    label = (region_ids % reg_count).astype(jnp.bfloat16)[:, None]
    pad = jnp.zeros((columns, extra_len - 3 * local_members - 1), jnp.bfloat16)
    extra = jnp.concatenate([f_hi, f_mid, f_lo, label, pad], axis=1)
    rows_major = jnp.transpose(ensemble, (2, 0, 1)).reshape(columns, row_len)
    rows = jnp.concatenate([rows_major, extra], axis=1)
    width = row_len + extra_len
    payload = jnp.take(rows, ordering, axis=0).reshape(n_space, n_member, slot_cols, width)
    received = lax.all_to_all(
        lax.all_to_all(payload, "member", split_axis=1, concat_axis=3, tiled=True),
        "space",
        split_axis=0,
        concat_axis=0,
        tiled=True,
    )
    gathered = received.reshape(own_cols, n_member, width)
    ens_part = gathered[:, :, :row_len].reshape(own_cols, members, tracers)
    ext = gathered[:, :, row_len:].astype(jnp.float32)
    lm = local_members
    fac = (ext[:, :, 0:lm] + ext[:, :, lm : 2 * lm] + ext[:, :, 2 * lm : 3 * lm]).reshape(
        own_cols, members
    )
    got_labels = ext[:, 0, 3 * lm].astype(jnp.int32)
    ens32 = ens_part.astype(jnp.float32)
    mean = jnp.sum(ens32, axis=1) / members
    anomaly = ((ens32 - mean[:, None, :]) * fac[:, :, None]).astype(jnp.bfloat16)
    accum = jnp.zeros((own_cols, members, tracers), jnp.float32)
    for region in range(reg_count):
        partial_prod = jnp.einsum(
            "jk,cjt->ckt", weights[region], anomaly, preferred_element_type=jnp.float32
        )
        accum = accum + jnp.where((got_labels == region)[:, None, None], partial_prod, 0.0)
    increment = accum.astype(jnp.bfloat16)
    result_rows = (mean[:, None, :] + increment.astype(jnp.float32)).astype(jnp.bfloat16)
    result_rows = result_rows.reshape(n_space, 1, slot_cols, members * tracers)
    halfway = lax.all_to_all(result_rows, "space", split_axis=0, concat_axis=0, tiled=True)
    returned = lax.all_to_all(halfway, "member", split_axis=3, concat_axis=1, tiled=True)
    restored = jnp.take(returned.reshape(columns, local_members * tracers), position, axis=0)
    analysis = jnp.transpose(restored.reshape(columns, local_members, tracers), (1, 2, 0))
    local_index = obs_cols - lax.axis_index("space") * columns
    picked = jnp.take(analysis, local_index, axis=2).astype(jnp.float32)
    obs_analysis = jnp.einsum("t,kto->ko", extinction, picked, precision=lax.Precision.HIGHEST)
    return (analysis, obs_analysis)


def solution(mesh):
    in_specs = (
        P("member", None, "space"),
        P("member", None),
        P("space", None, None),
        P("space"),
        P(),
        P("space"),
    )
    out_specs = (P("member", None, "space"), P("member", "space"))
    return jax.shard_map(local, mesh=mesh, in_specs=in_specs, out_specs=out_specs, check_vma=False)
```

profile of v0, /device:TPU:64, one launch (start us, length us, event | category | flops | bytes accessed | tf_op | source)
XLA Modules:
  0.0 318.0 jit_solution(428694375917716117)
XLA Ops:
  18.2 30.9 %all_to_all.43 = bf16[32,8,2,1664]{3,0,2,1:T(8,128)(2,1)S(1)} all-to-all(bf16[32,8,2,1664]{3,0,2,1:T(8,128)(2,1)S(1)} %copy_select_fusion), channel_id=1, replica_groups=mesh['member'=8,'space'=32] {'member'}, dimensions={1} | all-to-all | bytes 3407872 | tf_op jit(solution)/shard_map/all_to_all | solution.py:50
  50.5 49.5 %all_to_all.44 = bf16[32,1,2,13312]{3,2,1,0:T(2,128)(2,1)} all-to-all(bf16[32,1,2,13312]{3,2,1,0:T(2,128)(2,1)S(1)} %reshape.130), channel_id=1, replica_groups=mesh['member'=8,'space'=32] {'space'}, dimensions={0} | all-to-all | bytes 3407872 | tf_op jit(solution)/shard_map/all_to_all | solution.py:49
  100.0 4.2 %reshape.84 = bf16[64,8,1664]{2,1,0:T(8,128)(2,1)S(1)} reshape(bf16[32,1,2,13312]{3,2,1,0:T(2,128)(2,1)} %all_to_all.44) | data formatting | bytes 3407872 | tf_op jit(solution)/shard_map/reshape | solution.py:56
  104.2 4.7 %compare_reduce_fusion.3 = (pred[64]{0:T(512)(128)(4,1)S(1)}, pred[64]{0:T(512)(128)(4,1)S(1)}, pred[64]{0:T(512)(128)(4,1)S(1)}, pred[64]{0:T(512)(128)(4,1)S(1)}) fusion(f32[64,8,128]{2,1,0:T(8,128)S(1)} %slice_convert_fusion.1), kind=kLoop, calls=%fused_computation.34 | loop fusion | flops 320 | bytes 512 | tf_op jit(solution)/shard_map/eq | solution.py:72
  111.6 7.5 %reshape.87 = f32[64,256,48]{2,1,0:T(8,128)} reshape(f32[64,8,1536]{2,1,0:T(8,128)} %slice_convert_fusion) | data formatting | bytes 6291456 | tf_op jit(solution)/shard_map/convert_element_type | solution.py:64
  119.1 4.5 %reduce_sum.19 = f32[64,48]{1,0:T(8,128)S(1)} reduce(f32[64,256,48]{2,1,0:T(8,128)} %reshape.87, f32[]{:T(128)} %constant.89.clone.1), dimensions={1}, to_apply=%region_4.5 | reduce | flops 783360 | bytes 3158020 | tf_op jit(solution)/shard_map/reduce_sum | solution.py:65
  123.6 4.6 %mul.32 = f32[64,256,48]{2,1,0:T(8,128)} broadcast(f32[64,256]{1,0:T(8,128)S(1)} %copy.90), dimensions={0,1} | broadcast | bytes 3211264 | tf_op jit(solution)/shard_map/mul | solution.py:66
  128.2 9.0 %mul.33 = f32[64,8,1536]{2,1,0:T(8,128)} reshape(f32[64,256,48]{2,1,0:T(8,128)} %mul.32) | data formatting | bytes 6291456 | tf_op jit(solution)/shard_map/mul | solution.py:66
  137.2 3.8 %add.69 = f32[64,256,48]{2,1,0:T(8,128)} broadcast(f32[64,48]{1,0:T(8,128)S(1)} %broadcast_multiply_fusion), dimensions={0,2} | broadcast | bytes 3158016 | tf_op jit(solution)/shard_map/add | solution.py:74
  141.0 9.1 %add.70 = f32[64,8,1536]{2,1,0:T(8,128)} reshape(f32[64,256,48]{2,1,0:T(8,128)} %add.69) | data formatting | bytes 6291456 | tf_op jit(solution)/shard_map/add | solution.py:74
  150.1 3.6 %multiply_convert_fusion = bf16[64,8,1536]{2,1,0:T(8,128)(2,1)S(1)} fusion(f32[64,8,1536]{2,1,0:T(8,128)} %mul.33, f32[64,8,1536]{2,1,0:T(8,128)} %add.70, bf16[64,8,1664]{2,1,0:T(8,128)(2,1)S(1)} %reshape.84), kind=kLoop, calls=%fused_computation.7 | loop fusion | flops 3145728 | bytes 9437184 | tf_op jit(solution)/shard_map/convert_element_type | solution.py:66
  153.7 5.5 %convert_element_type.71 = bf16[64,256,48]{2,1,0:T(8,128)(2,1)} reshape(bf16[64,8,1536]{2,1,0:T(8,128)(2,1)S(1)} %multiply_convert_fusion) | data formatting | bytes 3145728 | tf_op jit(solution)/shard_map/convert_element_type | solution.py:66
  159.2 3.6 %fusion.5 = f32[64,48,256]{2,1,0:T(8,128)S(1)} fusion(bf16[64,256,48]{2,1,0:T(8,128)(2,1)} %convert_element_type.71, bf16[4,256,256]{2,1,0:T(8,128)(2,1)S(1)} %copy-done.3), kind=kOutput, calls=%fused_computation.20 | convolution fusion | flops 402653184 | bytes 4849664 | tf_op jit(solution)/shard_map/jk,cjt->ckt/dot_general | solution.py:69
  171.7 9.3 %reshape.85 = bf16[32,1,2,12288]{3,2,0,1:T(2,128)(2,1)S(1)} reshape(bf16[64,256,48]{2,1,0:T(8,128)(2,1)} %copy.95) | data formatting | bytes 3145728 | tf_op jit(solution)/shard_map/reshape | solution.py:75
  181.0 43.6 %all_to_all.45 = bf16[32,1,2,12288]{3,2,1,0:T(2,128)(2,1)S(1)} all-to-all(bf16[32,1,2,12288]{3,2,1,0:T(2,128)(2,1)S(1)} %bitcast.75), channel_id=1, replica_groups=mesh['member'=8,'space'=32] {'space'}, dimensions={0} | all-to-all | bytes 3145728 | tf_op jit(solution)/shard_map/all_to_all | solution.py:76
  224.6 11.1 %copy.97 = bf16[32,1,2,12288]{0,2,1,3:T(2,128)(2,1)} copy(bf16[32,1,2,12288]{3,2,1,0:T(2,128)(2,1)S(1)} %all_to_all.45) | data formatting | bytes 3145728 | tf_op jit(solution)/shard_map/all_to_all | solution.py:76
  235.7 9.5 %reshape.138 = bf16[8,2,49152]{2,1,0:T(2,128)(2,1)} reshape(bf16[12288,1,2,32]{3,2,1,0:T(2,128)(2,1)} %bitcast.72) | data formatting | bytes 3145728
  245.2 4.0 %all-to-all-start.3 = ((bf16[8,2,49152]{2,1,0:T(2,128)(2,1)}), bf16[8,2,49152]{2,1,0:T(2,128)(2,1)S(1)}, u32[]{:S(2)}, u32[]{:S(2)}) async-start(bf16[8,2,49152]{2,1,0:T(2,128)(2,1)} %reshape.138), calls=%async_computation.3 | async-start | bytes 3145728 | tf_op jit(solution)/shard_map/all_to_all | solution.py:77
  249.3 24.1 %all-to-all-done.3 = bf16[8,2,49152]{2,1,0:T(2,128)(2,1)S(1)} async-done(((bf16[8,2,49152]{2,1,0:T(2,128)(2,1)}), bf16[8,2,49152]{2,1,0:T(2,128)(2,1)S(1)}, u32[]{:S(2)}, u32[]{:S(2)}) %all-to-all-start.3) | async-done | bytes 1572896 | tf_op jit(solution)/shard_map/all_to_all | solution.py:77
  273.4 5.4 %reshape.139 = bf16[12288,1,2,32]{3,2,1,0:T(2,128)(2,1)} reshape(bf16[8,2,49152]{2,1,0:T(2,128)(2,1)S(1)} %all-to-all-done.3) | data formatting | bytes 3145728
  278.8 14.4 %copy.98 = bf16[32,1,2,8,1536]{4,2,3,0,1:T(2,128)(2,1)S(1)} copy(bf16[32,1,2,8,1536]{0,2,4,3,1:T(2,128)(2,1)} %bitcast.73) | data formatting | bytes 3145728 | tf_op jit(solution)/shard_map/all_to_all | solution.py:77
  296.8 6.5 %copy.100 = bf16[512,32,48]{2,1,0:T(8,128)(2,1)} copy(bf16[512,32,48]{0,2,1:T(8,128)(2,1)S(1)} %bitcast.76) | data formatting | bytes 3145728 | tf_op jit(solution)/shard_map/jit(_take)/gather | solution.py:78
  303.3 4.5 %select_bitcast_fusion = bf16[32,48,512]{1,0,2:T(8,128)(2,1)} fusion(bf16[512,32,48]{2,1,0:T(8,128)(2,1)} %copy.100, pred[512]{0:T(512)(128)(4,1)S(1)} %copy-done.8), kind=kLoop, calls=%fused_computation.4 | loop fusion | flops 786432 | bytes 3146240 | tf_op jit(solution)/shard_map/transpose | solution.py:79
  307.8 5.4 %copy.101 = bf16[32,48,512]{2,1,0:T(8,128)(2,1)} copy(bf16[32,48,512]{1,0,2:T(8,128)(2,1)} %select_bitcast_fusion) | data formatting | bytes 3145728
  (69 shorter events, 38.6 us)
Async XLA Ops:
  0.6 6.9 %copy-start = (f32[32,128]{1,0:T(8,128)S(1)}, f32[32,128]{1,0:T(8,128)}, u32[]{:S(2)}) copy-start(f32[32,128]{1,0:T(8,128)} %param.7) | copy-start | bytes 49156
  3.5 2.5 copy-start.6
  10.2 4.5 %copy-start.5 = (s32[1024]{0:T(1024)S(1)}, s32[1024]{0:T(1024)}, u32[]{:S(2)}) copy-start(s32[1024]{0:T(1024)} %pad_clamp_fusion.2) | copy-start | bytes 12292
  17.0 0.7 copy-start.4
  153.7 5.5 %copy-start.3 = (bf16[4,256,256]{2,1,0:T(8,128)(2,1)S(1)}, bf16[4,256,256]{2,1,0:T(8,128)(2,1)}, u32[]{:S(2)}) copy-start(bf16[4,256,256]{2,1,0:T(8,128)(2,1)} %param.8) | copy-start | bytes 1572868
  159.2 3.6 %copy-start.2 = (bf16[64,256,48]{2,1,0:T(8,128)(2,1)S(1)}, bf16[64,256,48]{2,1,0:T(8,128)(2,1)}, u32[]{:S(2)}) copy-start(bf16[64,256,48]{2,1,0:T(8,128)(2,1)} %convert_element_type.71) | copy-start | bytes 4718596
  245.2 4.0 %copy-start.7 = (s32[512]{0:T(512)S(1)}, s32[512]{0:T(512)}, u32[]{:S(2)}) copy-start(s32[512]{0:T(512)} %copy-done.6) | copy-start | bytes 6148
  245.2 4.0 %copy-start.10 = (s32[128]{0:T(128)S(1)}, s32[128]{0:T(128)}, u32[]{:S(2)}) copy-start(s32[128]{0:T(128)} %param.11) | copy-start | bytes 1540
  245.2 28.2 %all-to-all-start.3 = ((bf16[8,2,49152]{2,1,0:T(2,128)(2,1)}), bf16[8,2,49152]{2,1,0:T(2,128)(2,1)S(1)}, u32[]{:S(2)}, u32[]{:S(2)}) async-start(bf16[8,2,49152]{2,1,0:T(2,128)(2,1)} %reshape.138), calls=%async_computation.3 | async-start | bytes 3145728 | tf_op jit(solution)/shard_map/all_to_all | solution.py:77
  296.8 6.5 %copy-start.8 = (pred[512]{0:T(512)(128)(4,1)S(1)}, pred[512]{0:T(512)(128)(4,1)}, u32[]{:S(2)}) copy-start(pred[512]{0:T(512)(128)(4,1)} %get-tuple-element.16) | copy-start | bytes 1540
  307.8 8.5 %copy-start.9 = (f32[48]{0:T(128)S(1)}, f32[48]{0:T(128)}, u32[]{:S(2)}) copy-start(f32[48]{0:T(128)} %param.10) | copy-start | bytes 580
  307.8 10.1 %copy-start.1 = (f32[32,128]{1,0:T(8,128)S(1)}, f32[32,128]{1,0:T(8,128)}, u32[]{:S(2)}) copy-start(f32[32,128]{1,0:T(8,128)} %param.7) | copy-start | bytes 49156
where the time goes:
time: 320 us; the launch traced here: 318 us
  local copies, waits for them, and re-layouts  129 us (40%)
  blocking collectives  124 us (39%)
  waiting for transfers between devices  24.1 us (8%)
  other arithmetic  23.7 us (7%)
  matrix products  11.8 us (4%)
  starting transfers between devices  3.97 us (1%)
    all_to_all x1, blocking collectives, local(): lax.all_to_all(lax.all_to_all(payload, 'member', split_axis=1, concat_axi...  49.5 us
    all_to_all x1, blocking collectives, local(): lax.all_to_all(result_rows, 'space', split_axis=0, concat_axis=0, tiled=T...  43.6 us
    all_to_all x1, blocking collectives, local(): lax.all_to_all(payload, 'member', split_axis=1, concat_axis=3, tiled=True)  30.9 us
    all_to_all x1, waiting for transfers between devices, local(): lax.all_to_all(halfway, 'member', split_axis=3, concat_axis=1, tiled=True)  24.1 us
    unnamed x25, local copies, waits for them, and re-layouts  20.4 us
    all_to_all x1, local copies, waits for them, and re-layouts, local(): lax.all_to_all(halfway, 'member', split_axis=3, concat_axis=1, tiled=True)  14.4 us
    mul x3, local copies, waits for them, and re-layouts, local(): (ens32 - mean[:, None, :]) * fac[:, :, None]  13.7 us
    add x2, local copies, waits for them, and re-layouts, local(): mean[:, None, :] + increment.astype(jnp.float32)  12.8 us
  transfers between devices with their start and end apart: 1, of which 1 were waited for; matrix products, arithmetic and copies ran while one was open for 0% of the time, Pallas kernels for 0%

commit v1 on v0

--- a/solution.py
+++ b/solution.py
@@ -74,7 +74,12 @@
     result_rows = (mean[:, None, :] + increment.astype(jnp.float32)).astype(jnp.bfloat16)
     result_rows = result_rows.reshape(n_space, 1, slot_cols, members * tracers)
     halfway = lax.all_to_all(result_rows, "space", split_axis=0, concat_axis=0, tiled=True)
-    returned = lax.all_to_all(halfway, "member", split_axis=3, concat_axis=1, tiled=True)
+    returned = jnp.concatenate(
+        lax.all_to_all(
+            jnp.stack(jnp.split(halfway, lax.axis_size("member"), axis=3)), "member", 0, 0
+        ),
+        axis=1,
+    )
     restored = jnp.take(returned.reshape(columns, local_members * tracers), position, axis=0)
     analysis = jnp.transpose(restored.reshape(columns, local_members, tracers), (1, 2, 0))
     local_index = obs_cols - lax.axis_index("space") * columns

time: 320 us -> 287 us (0.90)
  local copies, waits for them, and re-layouts: 129 us -> 97 us
    all_to_all x2 -> x0, local copies, waits for them, and re-layouts: 25.5 us -> none  [the longest x1 14.4 us: local(): lax.all_to_all(halfway, 'member', split_axis=3, concat_axis=1, tiled=True)]
    unnamed x25 -> x30, local copies, waits for them, and re-layouts: 20.4 us -> 11.1 us
where the time goes in v1:
time: 287 us; the launch traced here: 286 us
  blocking collectives  124 us (43%)
  local copies, waits for them, and re-layouts  97 us (34%)
  waiting for transfers between devices  24.1 us (8%)
  other arithmetic  23.7 us (8%)
  matrix products  11.8 us (4%)
  starting transfers between devices  3.84 us (1%)
    all_to_all x1, blocking collectives, local(): lax.all_to_all(lax.all_to_all(payload, 'member', split_axis=1, concat_axi...  49.5 us
    all_to_all x1, blocking collectives, local(): lax.all_to_all(result_rows, 'space', split_axis=0, concat_axis=0, tiled=T...  43.6 us
    all_to_all x1, blocking collectives, local(): lax.all_to_all(payload, 'member', split_axis=1, concat_axis=3, tiled=True)  30.9 us
    all_to_all x1, waiting for transfers between devices, local(): lax.all_to_all(jnp.stack(jnp.split(halfway, lax.axis_size('member'), axis...  24.1 us
    mul x3, local copies, waits for them, and re-layouts, local(): (ens32 - mean[:, None, :]) * fac[:, :, None]  13.7 us
    add x2, local copies, waits for them, and re-layouts, local(): mean[:, None, :] + increment.astype(jnp.float32)  12.8 us
    unnamed x30, local copies, waits for them, and re-layouts  11.1 us
    gather x3, local copies, waits for them, and re-layouts, local(): jnp.take(returned.reshape(columns, local_members * tracers), position, ax...  9.38 us
  transfers between devices with their start and end apart: 1, of which 1 were waited for; matrix products, arithmetic and copies ran while one was open for 0% of the time, Pallas kernels for 0%

profile of v1, /device:TPU:64, one launch (start us, length us, event | category | flops | bytes accessed | tf_op | source)
XLA Modules:
  0.0 285.5 jit_solution(3586308878990334304)
XLA Ops:
  3.5 2.4 scatter_custom_fusion
  18.2 30.9 %all_to_all.33 = bf16[32,8,2,1664]{3,0,2,1:T(8,128)(2,1)S(1)} all-to-all(bf16[32,8,2,1664]{3,0,2,1:T(8,128)(2,1)S(1)} %copy_select_fusion), channel_id=1, replica_groups=mesh['member'=8,'space'=32] {'member'}, dimensions={1} | all-to-all | bytes 3407872 | tf_op jit(solution)/shard_map/all_to_all | solution.py:50
  50.5 49.5 %all_to_all.34 = bf16[32,1,2,13312]{3,2,1,0:T(2,128)(2,1)} all-to-all(bf16[32,1,2,13312]{3,2,1,0:T(2,128)(2,1)S(1)} %reshape.129), channel_id=1, replica_groups=mesh['member'=8,'space'=32] {'space'}, dimensions={0} | all-to-all | bytes 3407872 | tf_op jit(solution)/shard_map/all_to_all | solution.py:49
  100.0 4.2 %reshape.83 = bf16[64,8,1664]{2,1,0:T(8,128)(2,1)S(1)} reshape(bf16[32,1,2,13312]{3,2,1,0:T(2,128)(2,1)} %all_to_all.34) | data formatting | bytes 3407872 | tf_op jit(solution)/shard_map/reshape | solution.py:56
  104.2 4.7 %compare_reduce_fusion.3 = (pred[64]{0:T(512)(128)(4,1)S(1)}, pred[64]{0:T(512)(128)(4,1)S(1)}, pred[64]{0:T(512)(128)(4,1)S(1)}, pred[64]{0:T(512)(128)(4,1)S(1)}) fusion(f32[64,8,128]{2,1,0:T(8,128)S(1)} %slice_convert_fusion.1), kind=kLoop, calls=%fused_computation.50 | loop fusion | flops 320 | bytes 512 | tf_op jit(solution)/shard_map/eq | solution.py:72
  111.6 7.5 %reshape.86 = f32[64,256,48]{2,1,0:T(8,128)} reshape(f32[64,8,1536]{2,1,0:T(8,128)} %slice_convert_fusion) | data formatting | bytes 6291456 | tf_op jit(solution)/shard_map/convert_element_type | solution.py:64
  119.1 4.5 %reduce_sum.19 = f32[64,48]{1,0:T(8,128)S(1)} reduce(f32[64,256,48]{2,1,0:T(8,128)} %reshape.86, f32[]{:T(128)} %constant.89.clone.1), dimensions={1}, to_apply=%region_4.5 | reduce | flops 783360 | bytes 3158020 | tf_op jit(solution)/shard_map/reduce_sum | solution.py:65
  123.6 4.6 %mul.32 = f32[64,256,48]{2,1,0:T(8,128)} broadcast(f32[64,256]{1,0:T(8,128)S(1)} %copy.74), dimensions={0,1} | broadcast | bytes 3211264 | tf_op jit(solution)/shard_map/mul | solution.py:66
  128.2 9.0 %mul.33 = f32[64,8,1536]{2,1,0:T(8,128)} reshape(f32[64,256,48]{2,1,0:T(8,128)} %mul.32) | data formatting | bytes 6291456 | tf_op jit(solution)/shard_map/mul | solution.py:66
  137.2 3.8 %add.69 = f32[64,256,48]{2,1,0:T(8,128)} broadcast(f32[64,48]{1,0:T(8,128)S(1)} %broadcast_multiply_fusion), dimensions={0,2} | broadcast | bytes 3158016 | tf_op jit(solution)/shard_map/add | solution.py:74
  141.0 9.1 %add.70 = f32[64,8,1536]{2,1,0:T(8,128)} reshape(f32[64,256,48]{2,1,0:T(8,128)} %add.69) | data formatting | bytes 6291456 | tf_op jit(solution)/shard_map/add | solution.py:74
  150.0 3.6 %multiply_convert_fusion = bf16[64,8,1536]{2,1,0:T(8,128)(2,1)S(1)} fusion(f32[64,8,1536]{2,1,0:T(8,128)} %mul.33, f32[64,8,1536]{2,1,0:T(8,128)} %add.70, bf16[64,8,1664]{2,1,0:T(8,128)(2,1)S(1)} %reshape.83), kind=kLoop, calls=%fused_computation.7 | loop fusion | flops 3145728 | bytes 9437184 | tf_op jit(solution)/shard_map/convert_element_type | solution.py:66
  153.7 5.5 %convert_element_type.71 = bf16[64,256,48]{2,1,0:T(8,128)(2,1)} reshape(bf16[64,8,1536]{2,1,0:T(8,128)(2,1)S(1)} %multiply_convert_fusion) | data formatting | bytes 3145728 | tf_op jit(solution)/shard_map/convert_element_type | solution.py:66
  159.2 3.6 %fusion.13 = f32[64,48,256]{2,1,0:T(8,128)S(1)} fusion(bf16[64,256,48]{2,1,0:T(8,128)(2,1)} %convert_element_type.71, bf16[4,256,256]{2,1,0:T(8,128)(2,1)S(1)} %copy-done.3), kind=kOutput, calls=%fused_computation.36 | convolution fusion | flops 402653184 | bytes 4849664 | tf_op jit(solution)/shard_map/jk,cjt->ckt/dot_general | solution.py:69
  165.4 3.2 %fusion = bf16[64,256,48]{1,2,0:T(8,128)(2,1)S(1)} fusion(f32[64,48]{1,0:T(8,128)S(1)} %broadcast_multiply_fusion, bf16[64,256,48]{2,1,0:T(8,128)(2,1)S(1)} %copy-done.2, pred[64]{0:T(512)(128)(4,1)S(1)} %get-tuple-element.11, f32[64,48,256]{2,1,0:T(8,128)S(1)} %fusion.13, pred[64]{0:T(512)(128)(4,1)S(1)} %get-tuple-element.10, ...), kind=kOutput, calls=%fused_computation.9 | convolution fusion | flops 411303936 | bytes 12726528 | tf_op jit(solution)/shard_map/jk,cjt->ckt/dot_general | solution.py:69
  168.6 3.2 %copy.79 = bf16[64,256,48]{2,1,0:T(8,128)(2,1)} copy(bf16[64,256,48]{1,2,0:T(8,128)(2,1)S(1)} %fusion) | data formatting | bytes 3145728 | tf_op jit(solution)/shard_map/convert_element_type | solution.py:74
  171.7 9.3 %reshape.84 = bf16[32,1,2,12288]{3,2,0,1:T(2,128)(2,1)S(1)} reshape(bf16[64,256,48]{2,1,0:T(8,128)(2,1)} %copy.79) | data formatting | bytes 3145728 | tf_op jit(solution)/shard_map/reshape | solution.py:75
  181.0 43.6 %all_to_all.35 = bf16[32,1,2,12288]{3,2,1,0:T(2,128)(2,1)S(1)} all-to-all(bf16[32,1,2,12288]{3,2,1,0:T(2,128)(2,1)S(1)} %bitcast.117), channel_id=1, replica_groups=mesh['member'=8,'space'=32] {'space'}, dimensions={0} | all-to-all | bytes 3145728 | tf_op jit(solution)/shard_map/all_to_all | solution.py:76
  231.1 3.8 %all-to-all-start.3 = ((bf16[8,32,1,2,1536]{4,3,1,2,0:T(2,128)(2,1)}), bf16[8,32,1,2,1536]{4,3,1,2,0:T(2,128)(2,1)S(1)}, u32[]{:S(2)}, u32[]{:S(2)}) async-start(bf16[8,32,1,2,1536]{4,3,1,2,0:T(2,128)(2,1)} %fusion.4), calls=%async_computation.3 | async-start | bytes 3145728 | tf_op jit(solution)/shard_map/all_to_all | solution.py:78
  235.1 24.1 %all-to-all-done.3 = bf16[8,32,1,2,1536]{4,3,1,2,0:T(2,128)(2,1)S(1)} async-done(((bf16[8,32,1,2,1536]{4,3,1,2,0:T(2,128)(2,1)}), bf16[8,32,1,2,1536]{4,3,1,2,0:T(2,128)(2,1)S(1)}, u32[]{:S(2)}, u32[]{:S(2)}) %all-to-all-start.3) | async-done | bytes 1572896 | tf_op jit(solution)/shard_map/all_to_all | solution.py:78
  264.3 6.5 %copy.90 = bf16[512,32,48]{2,1,0:T(8,128)(2,1)} copy(bf16[512,32,48]{0,2,1:T(8,128)(2,1)S(1)} %bitcast.118) | data formatting | bytes 3145728 | tf_op jit(solution)/shard_map/jit(_take)/gather | solution.py:83
  270.9 4.5 %select_bitcast_fusion = bf16[32,48,512]{1,0,2:T(8,128)(2,1)} fusion(bf16[512,32,48]{2,1,0:T(8,128)(2,1)} %copy.90, pred[512]{0:T(512)(128)(4,1)S(1)} %copy-done.8), kind=kLoop, calls=%fused_computation.4 | loop fusion | flops 786432 | bytes 3146240 | tf_op jit(solution)/shard_map/transpose | solution.py:84
  275.4 5.3 %copy.91 = bf16[32,48,512]{2,1,0:T(8,128)(2,1)} copy(bf16[32,48,512]{1,0,2:T(8,128)(2,1)} %select_bitcast_fusion) | data formatting | bytes 3145728
  280.7 3.0 %gather_fusion.2 = bf16[128,32,48]{2,1,0:T(8,128)(2,1)S(1)} fusion(bf16[32,48,512]{1,0,2:T(8,128)(2,1)} %select_bitcast_fusion, s32[1024]{0:T(1024)S(1)} %get-tuple-element.21), kind=kCustom, calls=%fused_computation.2 | custom fusion | bytes 786944 | tf_op jit(solution)/shard_map/jit(_take)/gather | solution.py:86
  (73 shorter events, 35.0 us)
Async XLA Ops:
  0.6 6.9 %copy-start = (f32[32,128]{1,0:T(8,128)S(1)}, f32[32,128]{1,0:T(8,128)}, u32[]{:S(2)}) copy-start(f32[32,128]{1,0:T(8,128)} %param.7) | copy-start | bytes 49156
  3.5 2.5 copy-start.6
  12.6 2.1 copy-start.5
  17.0 0.7 copy-start.4
  153.7 5.5 %copy-start.3 = (bf16[4,256,256]{2,1,0:T(8,128)(2,1)S(1)}, bf16[4,256,256]{2,1,0:T(8,128)(2,1)}, u32[]{:S(2)}) copy-start(bf16[4,256,256]{2,1,0:T(8,128)(2,1)} %param.8) | copy-start | bytes 1572868
  159.2 3.6 %copy-start.2 = (bf16[64,256,48]{2,1,0:T(8,128)(2,1)S(1)}, bf16[64,256,48]{2,1,0:T(8,128)(2,1)}, u32[]{:S(2)}) copy-start(bf16[64,256,48]{2,1,0:T(8,128)(2,1)} %convert_element_type.71) | copy-start | bytes 4718596
  230.3 4.7 %copy-start.10 = (s32[128]{0:T(128)S(1)}, s32[128]{0:T(128)}, u32[]{:S(2)}) copy-start(s32[128]{0:T(128)} %param.11) | copy-start | bytes 1540
  230.3 4.7 %copy-start.7 = (s32[512]{0:T(512)S(1)}, s32[512]{0:T(512)}, u32[]{:S(2)}) copy-start(s32[512]{0:T(512)} %copy-done.6) | copy-start | bytes 6148
  231.1 28.0 %all-to-all-start.3 = ((bf16[8,32,1,2,1536]{4,3,1,2,0:T(2,128)(2,1)}), bf16[8,32,1,2,1536]{4,3,1,2,0:T(2,128)(2,1)S(1)}, u32[]{:S(2)}, u32[]{:S(2)}) async-start(bf16[8,32,1,2,1536]{4,3,1,2,0:T(2,128)(2,1)} %fusion.4), calls=%async_computation.3 | async-start | bytes 3145728 | tf_op jit(solution)/shard_map/all_to_all | solution.py:78
  264.3 6.5 %copy-start.8 = (pred[512]{0:T(512)(128)(4,1)S(1)}, pred[512]{0:T(512)(128)(4,1)}, u32[]{:S(2)}) copy-start(pred[512]{0:T(512)(128)(4,1)} %get-tuple-element.14) | copy-start | bytes 1540
  280.7 3.2 %copy-start.9 = (f32[48]{0:T(128)S(1)}, f32[48]{0:T(128)}, u32[]{:S(2)}) copy-start(f32[48]{0:T(128)} %param.10) | copy-start | bytes 580
  280.7 4.8 %copy-start.1 = (f32[32,128]{1,0:T(8,128)S(1)}, f32[32,128]{1,0:T(8,128)}, u32[]{:S(2)}) copy-start(f32[32,128]{1,0:T(8,128)} %param.7) | copy-start | bytes 49156
